TPU v7x, 32 devices: a whole 2x2x4 slice. The times are simulated.
32 devices in a mesh: section: 4 (over z), dp: 2 (over core), seq: 4 (over y, x).
Axes of the slice: x: 2, y: 2, z: 4, core: 2. Of those that a mesh axis runs over, the one named last changes fastest.
Arguments:
- qkv: bfloat16 [4, 4, 256, 6144], P('section', 'dp', 'seq'), may hold values from -5 to 5
- stream_lengths: int32 [4, 4], P('section'), may hold values from 1 to 192, 256 in all within a row
- doc_lengths: int32 [4, 4, 8], P('section'), may hold values from 1 to 128, 256 in all within a row
- hand_over: int32 [4, 2], P('section'), may hold values from 0 to 1
Outputs:
- handoff: bfloat16 [4, 4, 256, 4096], P('section', 'dp', 'seq')
Inputs may be any that keep to these rules, and one draw needn't show every extreme that they name: `stream_lengths`: each entry is the length of one row; the 4 entries of one section, taken together, sum to 256, and in each section one entry is exactly the most.
All inputs are finite; a program needn't handle non-finite values.
Results may differ from a plain program's by a relative error of at most 0.0013.
Values may be sent and summed in bfloat16 or wider, within the bound.
No kernel may reach another device: no remote copies, remote signals or barrier semaphores. Data moves between devices by JAX's collectives and lax.ppermute only.
A program may use at most 64 MiB of HBM per device.

v0:
```python
import jax
import jax.numpy as jnp
from jax import lax
from jax.sharding import PartitionSpec as P

H = 32
HD = 128
KV_HEADS = 8
D = 4096
RPR = 2


def swapped(block, axis, distance):
    count = lax.axis_size(axis)
    route = []
    for low in range(count):
        high = low | 1 << distance
        if high != low and high < count:
            route += [(low, high), (high, low)]
    return lax.ppermute(block, axis, route)


def passed_along(value, axis, steps):
    count = lax.axis_size(axis)
    pairs = [(source, (source + steps) % count) for source in range(count)]
    return lax.ppermute(value, axis, pairs)


def attend(row_data, row_ids, stream_lengths, doc_ends, seq_count):
    seg_len = row_data.shape[1]
    length = seg_len * seq_count
    heads_dev = H // seq_count
    group_size = H // KV_HEADS
    kv_dev = max(1, heads_dev // group_size)
    copies = max(1, group_size // heads_dev)
    group_local = heads_dev // kv_dev
    q_width = H * HD
    key_value_width = KV_HEADS * HD
    query_send = row_data[..., :q_width].reshape(RPR, seg_len, seq_count, heads_dev * HD)
    key_portion = row_data[..., q_width : q_width + key_value_width]
    value_part = row_data[..., q_width + key_value_width :]
    key_send = jnp.repeat(key_portion.reshape(RPR, seg_len, KV_HEADS, HD), copies, axis=2).reshape(
        RPR, seg_len, seq_count, kv_dev * HD
    )
    value_send = jnp.repeat(value_part.reshape(RPR, seg_len, KV_HEADS, HD), copies, axis=2).reshape(
        RPR, seg_len, seq_count, kv_dev * HD
    )
    query_heads, kv_heads = (
        lax.all_to_all(query_send, "seq", split_axis=2, concat_axis=1, tiled=True),
        lax.all_to_all(
            jnp.concatenate([key_send, value_send], axis=3),
            "seq",
            split_axis=2,
            concat_axis=1,
            tiled=True,
        ),
    )
    key_block = kv_heads[:, :, 0, : kv_dev * HD]
    value_block = kv_heads[:, :, 0, kv_dev * HD :]
    query_tile_rows = query_heads[:, :, 0, :]
    positions = jnp.arange(length, dtype=jnp.int32)
    row_match = (
        jnp.arange(doc_ends.shape[0], dtype=jnp.int32)[None, :] == row_ids[:, None]
    ).astype(jnp.int32)
    ends_rows = jnp.sum(row_match[:, :, None] * doc_ends[None, :, :], axis=1)
    lengths_rows = jnp.sum(row_match * stream_lengths[None, :], axis=1)
    doc_index = jnp.sum(
        (positions[None, :, None] >= ends_rows[:, None, :]).astype(jnp.int32), axis=2
    )
    causal = positions[:, None] >= positions[None, :]
    score_scale = HD ** (-0.5)
    results = []
    for slot_index in range(RPR):
        allowed = causal & (doc_index[slot_index][:, None] == doc_index[slot_index][None, :])
        query_row = query_tile_rows[slot_index].reshape(length, kv_dev, group_local, HD)
        key_row = key_block[slot_index].reshape(length, kv_dev, HD)
        value_row = value_block[slot_index].reshape(length, kv_dev, HD)
        scores = (
            jnp.einsum("qkgd,skd->kgqs", query_row, key_row, preferred_element_type=jnp.float32)
            * score_scale
        )
        row_top = jnp.max(jnp.where(allowed, scores, -jnp.inf), axis=-1, keepdims=True)
        weights = jnp.where(allowed, jnp.exp(scores - row_top), 0.0)
        row_total = jnp.sum(weights, axis=-1)
        rounded = weights.astype(jnp.bfloat16)
        summed = jnp.einsum(
            "kgqs,skd->qkgd", rounded, value_row, preferred_element_type=jnp.float32
        )
        result = summed / jnp.transpose(row_total, (2, 0, 1))[..., None]
        valid = (positions < lengths_rows[slot_index]).astype(jnp.float32)
        result = result * valid[:, None, None, None]
        results.append(result.reshape(length, heads_dev * HD).astype(jnp.bfloat16))
    return jnp.stack(results, axis=0)


def shards(qkv, stream_lengths, doc_lengths, hand_over):
    seq_count = lax.axis_size("seq")
    replica = lax.axis_index("dp")
    partner = jnp.bitwise_xor(replica, 1)
    handed = lax.dynamic_index_in_dim(hand_over[0], replica, 0, keepdims=False)
    partner_handed = lax.dynamic_index_in_dim(hand_over[0], partner, 0, keepdims=False)
    own_rows = qkv[0]
    seg_len = own_rows.shape[1]
    doc_ends = jnp.cumsum(doc_lengths[0], axis=1)
    lengths_all = stream_lengths[0]
    given = lax.dynamic_index_in_dim(own_rows, handed, 0, keepdims=True)
    kept = lax.dynamic_index_in_dim(own_rows, 1 - handed, 0, keepdims=True)
    received = swapped(given, "dp", 0)
    row_ids = jnp.stack([2 * replica + 1 - handed, 2 * partner + partner_handed])
    attention_output = attend(
        jnp.concatenate([kept, received], axis=0), row_ids, lengths_all, doc_ends, seq_count
    )
    grouped = attention_output.reshape(RPR, seq_count, seg_len, attention_output.shape[2])
    tokens = lax.all_to_all(grouped, "seq", split_axis=1, concat_axis=3, tiled=True)
    tokens = passed_along(tokens, "section", 1)
    return tokens.reshape(1, RPR, seg_len, D)


def solution(mesh):
    return jax.shard_map(
        shards,
        mesh=mesh,
        in_specs=(
            P("section", "dp", "seq", None),
            P("section", None),
            P("section", None, None),
            P("section", None),
        ),
        out_specs=P("section", "dp", "seq", None),
        check_vma=False,
    )
```

profile of v0, /device:TPU:0, one launch (start us, length us, event | category | flops | bytes accessed | tf_op | source)
XLA Modules:
  0.0 89.6 jit_solution(12574448168181887721)
XLA Ops:
  0.0 1.4 %constant_dynamic-slice_fusion = (s32[1,1]{1,0:T(1,128)}, s32[1,1]{1,0:T(1,128)}) fusion(s32[1,2]{1,0:T(1,128)} %param.7, s32[]{:T(128)S(6)} %select_n.30, s32[]{:T(128)S(6)} %select_n.27), kind=kLoop, calls=%fused_computation.53 | loop fusion | bytes 24 | tf_op jit(solution)/shard_map/jit(dynamic_index_in_dim)/dynamic_slice | solution.py:101
  4.9 1.5 %dynamic-slice_bitcast_fusion.1 = (bf16[1,64,6144]{2,1,0:T(8,128)(2,1)S(1)}, bf16[1,64,6144]{2,1,0:T(8,128)(2,1)S(1)}) fusion(bf16[1,2,64,6144]{3,2,1,0:T(8,128)(2,1)} %param.4, s32[]{:T(128)S(6)} %select_n.28, s32[]{:T(128)S(6)} %select_n.29), kind=kLoop, calls=%fused_computation.34 | loop fusion | bytes 3145736 | tf_op jit(solution)/shard_map/jit(dynamic_index_in_dim)/dynamic_slice | solution.py:107
  6.3 0.6 collective-permute-start
  8.7 0.7 fusion.38
  9.4 0.6 compare_convert_fusion.1
  10.9 0.9 copy.54
  11.8 4.7 %all-to-all-start = ((bf16[2,64,4,512]{3,1,0,2:T(8,128)(2,1)}), bf16[2,64,4,512]{3,1,0,2:T(8,128)(2,1)S(1)}, u32[]{:S(2)}, u32[]{:S(2)}) async-start(bf16[2,64,4,512]{3,1,0,2:T(8,128)(2,1)} %copy.54), calls=%async_computation | async-start | bytes 1048576 | tf_op jit(solution)/shard_map/all_to_all | solution.py:50
  16.6 1.1 %copy.88 = bf16[2,8,4,8,1024]{4,3,1,0,2:T(8,128)(2,1)} copy(bf16[2,8,4,8,1024]{4,3,2,1,0:T(8,128)(2,1)S(1)} %bitcast.113) | data formatting | bytes 2097152 | tf_op jit(solution)/shard_map/reshape | solution.py:39
  17.7 7.5 %all-to-all-done = bf16[2,64,4,512]{3,1,0,2:T(8,128)(2,1)S(1)} async-done(((bf16[2,64,4,512]{3,1,0,2:T(8,128)(2,1)}), bf16[2,64,4,512]{3,1,0,2:T(8,128)(2,1)S(1)}, u32[]{:S(2)}, u32[]{:S(2)}) %all-to-all-start) | async-done | bytes 524320 | tf_op jit(solution)/shard_map/all_to_all | solution.py:50
  25.2 3.5 %all-to-all-start.1 = ((bf16[2,64,4,1024]{3,1,0,2:T(8,128)(2,1)}), bf16[2,64,4,1024]{3,1,0,2:T(8,128)(2,1)S(1)}, u32[]{:S(2)}, u32[]{:S(2)}) async-start(bf16[2,64,4,1024]{3,1,0,2:T(8,128)(2,1)} %bitcast.111), calls=%async_computation.1 | async-start | bytes 2097152 | tf_op jit(solution)/shard_map/all_to_all | solution.py:49
  28.7 0.7 compare_convert_fusion
  30.2 12.0 %all-to-all-done.1 = bf16[2,64,4,1024]{3,1,0,2:T(8,128)(2,1)S(1)} async-done(((bf16[2,64,4,1024]{3,1,0,2:T(8,128)(2,1)}), bf16[2,64,4,1024]{3,1,0,2:T(8,128)(2,1)S(1)}, u32[]{:S(2)}, u32[]{:S(2)}) %all-to-all-start.1) | async-done | bytes 1048608 | tf_op jit(solution)/shard_map/all_to_all | solution.py:49
  42.2 0.4 reshape_squeeze.20
  42.6 0.5 fusion.26
  43.1 0.9 fusion.40
  44.6 0.4 convert_element_type.63
  45.0 0.4 reshape_squeeze.23
  45.4 0.5 fusion.24
  45.8 0.9 fusion.39
  47.4 0.4 convert_element_type.67
  47.9 16.1 %all_to_all.51 = bf16[2,4,64,1024]{3,2,0,1:T(8,128)(2,1)S(1)} all-to-all(bf16[2,4,64,1024]{3,2,0,1:T(8,128)(2,1)S(1)} %copy.69), channel_id=1, replica_groups=mesh['section'=4,'dp'=2,'seq'=4] {'seq'}, dimensions={1} | all-to-all | bytes 2097152 | tf_op jit(solution)/shard_map/all_to_all | solution.py:114
  64.1 1.6 %collective-permute-start.1 = (bf16[2,1,64,4096]{3,2,0,1:T(8,128)(2,1)S(1)}, bf16[2,1,64,4096]{3,2,0,1:T(8,128)(2,1)S(1)}, u32[]{:S(2)}, u32[]{:S(2)}) collective-permute-start(bf16[2,1,64,4096]{3,2,0,1:T(8,128)(2,1)S(1)} %bitcast.116), channel_id=1, source_target_pairs={{0,8},{8,16},{16,24},{24,0},{1,9},{9,17},{17,25},{25,1},{2,10},{10... | collective-permute-start | bytes 3145736 | tf_op jit(solution)/shard_map/ppermute | solution.py:26
  65.7 22.9 %collective-permute-done.1 = bf16[2,1,64,4096]{3,2,0,1:T(8,128)(2,1)S(1)} collective-permute-done((bf16[2,1,64,4096]{3,2,0,1:T(8,128)(2,1)S(1)}, bf16[2,1,64,4096]{3,2,0,1:T(8,128)(2,1)S(1)}, u32[]{:S(2)}, u32[]{:S(2)}) %collective-permute-start.1) | collective-permute-done | bytes 1048608 | tf_op jit(solution)/shard_map/ppermute | solution.py:26
  88.7 1.0 %copy.90 = bf16[1,2,64,4096]{3,2,1,0:T(8,128)(2,1)} copy(bf16[1,2,64,4096]{3,2,1,0:T(8,128)(2,1)S(1)} %bitcast.117) | data formatting | bytes 2097152
  (33 shorter events, 3.7 us)
Async XLA Ops:
  0.0 7.6 %copy-start = (s32[1,4,8]{2,1,0:T(4,128)S(1)}, s32[1,4,8]{2,1,0:T(4,128)}, u32[]{:S(2)}) copy-start(s32[1,4,8]{2,1,0:T(4,128)} %param.6) | copy-start | bytes 388
  0.0 8.5 %copy-start.1 = (s32[1,4]{1,0:T(1,128)S(1)}, s32[1,4]{1,0:T(1,128)}, u32[]{:S(2)}) copy-start(s32[1,4]{1,0:T(1,128)} %param.5) | copy-start | bytes 52
  6.3 3.9 %collective-permute-start = (bf16[1,64,6144]{2,1,0:T(8,128)(2,1)S(1)}, bf16[1,64,6144]{2,1,0:T(8,128)(2,1)S(1)}, u32[]{:S(2)}, u32[]{:S(2)}) collective-permute-start(bf16[1,64,6144]{2,1,0:T(8,128)(2,1)S(1)} %get-tuple-element.8), channel_id=1, source_target_pairs={{0,4},{4,0},{1,5},{5,1},{2,6},{6,2},{3,7},{7,3},{8,12},{12,8},{9,1... | collective-permute-start | bytes 2359304 | tf_op jit(solution)/shard_map/ppermute | solution.py:20
  11.8 13.4 %all-to-all-start = ((bf16[2,64,4,512]{3,1,0,2:T(8,128)(2,1)}), bf16[2,64,4,512]{3,1,0,2:T(8,128)(2,1)S(1)}, u32[]{:S(2)}, u32[]{:S(2)}) async-start(bf16[2,64,4,512]{3,1,0,2:T(8,128)(2,1)} %copy.54), calls=%async_computation | async-start | bytes 1048576 | tf_op jit(solution)/shard_map/all_to_all | solution.py:50
  25.2 16.9 %all-to-all-start.1 = ((bf16[2,64,4,1024]{3,1,0,2:T(8,128)(2,1)}), bf16[2,64,4,1024]{3,1,0,2:T(8,128)(2,1)S(1)}, u32[]{:S(2)}, u32[]{:S(2)}) async-start(bf16[2,64,4,1024]{3,1,0,2:T(8,128)(2,1)} %bitcast.111), calls=%async_computation.1 | async-start | bytes 2097152 | tf_op jit(solution)/shard_map/all_to_all | solution.py:49
  64.1 24.6 %collective-permute-start.1 = (bf16[2,1,64,4096]{3,2,0,1:T(8,128)(2,1)S(1)}, bf16[2,1,64,4096]{3,2,0,1:T(8,128)(2,1)S(1)}, u32[]{:S(2)}, u32[]{:S(2)}) collective-permute-start(bf16[2,1,64,4096]{3,2,0,1:T(8,128)(2,1)S(1)} %bitcast.116), channel_id=1, source_target_pairs={{0,8},{8,16},{16,24},{24,0},{1,9},{9,17},{17,25},{25,1},{2,10},{10... | collective-permute-start | bytes 3145736 | tf_op jit(solution)/shard_map/ppermute | solution.py:26
where the time goes:
time: 90 us; the launch traced here: 89.6 us
  waiting for transfers between devices  42.4 us (47%)
  blocking collectives  16.1 us (18%)
  starting transfers between devices  10.4 us (12%)
  local copies, waits for them, and re-layouts  9.62 us (11%)
  between operations  5.03 us (6%)
  other arithmetic  4.47 us (5%)
  matrix products  1.61 us (2%)
    ppermute x1, waiting for transfers between devices, passed_along(): return lax.ppermute(value, axis, pairs)  22.9 us
    all_to_all x1, blocking collectives, shards(): lax.all_to_all(grouped, 'seq', split_axis=1, concat_axis=3, tiled=True)  16.1 us
    all_to_all x1, waiting for transfers between devices, attend(): lax.all_to_all(query_send, 'seq', split_axis=2, concat_axis=1, tiled=True)  12 us
    all_to_all x1, waiting for transfers between devices, attend(): lax.all_to_all(jnp.concatenate([key_send, value_send], axis=3), 'seq', sp...  7.52 us
    all_to_all x1, starting transfers between devices, attend(): lax.all_to_all(jnp.concatenate([key_send, value_send], axis=3), 'seq', sp...  4.71 us
    all_to_all x1, starting transfers between devices, attend(): lax.all_to_all(query_send, 'seq', split_axis=2, concat_axis=1, tiled=True)  3.52 us
  transfers between devices with their start and end apart: 4, of which 3 were waited for; matrix products, arithmetic and copies ran while one was open for 5% of the time, Pallas kernels for 0%

commit v1 on v0

--- a/solution.py
+++ b/solution.py
@@ -8,6 +8,12 @@
 KV_HEADS = 8
 D = 4096
 RPR = 2
+
+
+def form_target(x_local):
+    reached = jnp.stack(jnp.split(x_local, lax.axis_size("seq"), axis=2))
+    small = lax.all_to_all(reached, axis_name="seq", split_axis=0, concat_axis=0)
+    return jnp.concatenate(small, axis=1)
 
 
 def swapped(block, axis, distance):
@@ -47,13 +53,7 @@
     )
     query_heads, kv_heads = (
         lax.all_to_all(query_send, "seq", split_axis=2, concat_axis=1, tiled=True),
-        lax.all_to_all(
-            jnp.concatenate([key_send, value_send], axis=3),
-            "seq",
-            split_axis=2,
-            concat_axis=1,
-            tiled=True,
-        ),
+        form_target(jnp.concatenate([key_send, value_send], axis=3)),
     )
     key_block = kv_heads[:, :, 0, : kv_dev * HD]
     value_block = kv_heads[:, :, 0, kv_dev * HD :]

time: 90 us -> 90.9 us (1.010)
  no operation moved by 1% of the time
where the time goes in v1:
time: 90.9 us; the launch traced here: 90.5 us
  waiting for transfers between devices  42.4 us (47%)
  blocking collectives  16.1 us (18%)
  starting transfers between devices  10.4 us (11%)
  local copies, waits for them, and re-layouts  9.82 us (11%)
  other arithmetic  5.1 us (6%)
  between operations  5.06 us (6%)
  matrix products  1.61 us (2%)
    ppermute x1, waiting for transfers between devices, passed_along(): return lax.ppermute(value, axis, pairs)  22.9 us
    all_to_all x1, blocking collectives, shards(): lax.all_to_all(grouped, 'seq', split_axis=1, concat_axis=3, tiled=True)  16.1 us
    all_to_all x1, waiting for transfers between devices, attend(): lax.all_to_all(query_send, 'seq', split_axis=2, concat_axis=1, tiled=True)  12 us
    all_to_all x1, waiting for transfers between devices, form_target(): lax.all_to_all(reached, axis_name='seq', split_axis=0, concat_axis=0)  7.52 us
    all_to_all x1, starting transfers between devices, form_target(): lax.all_to_all(reached, axis_name='seq', split_axis=0, concat_axis=0)  4.71 us
    all_to_all x1, starting transfers between devices, attend(): lax.all_to_all(query_send, 'seq', split_axis=2, concat_axis=1, tiled=True)  3.52 us
  transfers between devices with their start and end apart: 4, of which 3 were waited for; matrix products, arithmetic and copies ran while one was open for 5% of the time, Pallas kernels for 0%

profile of v1, /device:TPU:0, one launch (start us, length us, event | category | flops | bytes accessed | tf_op | source)
XLA Modules:
  0.0 90.5 jit_solution(7274897276272407798)
XLA Ops:
  0.0 1.4 %constant_dynamic-slice_fusion = (s32[1,1]{1,0:T(1,128)}, s32[1,1]{1,0:T(1,128)}) fusion(s32[1,2]{1,0:T(1,128)} %param.7, s32[]{:T(128)S(6)} %select_n.30, s32[]{:T(128)S(6)} %select_n.27), kind=kLoop, calls=%fused_computation.59 | loop fusion | bytes 24 | tf_op jit(solution)/shard_map/jit(dynamic_index_in_dim)/dynamic_slice | solution.py:101
  4.9 1.5 %dynamic-slice_bitcast_fusion.1 = (bf16[1,64,6144]{2,1,0:T(8,128)(2,1)S(1)}, bf16[1,64,6144]{2,1,0:T(8,128)(2,1)S(1)}) fusion(bf16[1,2,64,6144]{3,2,1,0:T(8,128)(2,1)} %param.4, s32[]{:T(128)S(6)} %select_n.28, s32[]{:T(128)S(6)} %select_n.29), kind=kLoop, calls=%fused_computation.34 | loop fusion | bytes 3145736 | tf_op jit(solution)/shard_map/jit(dynamic_index_in_dim)/dynamic_slice | solution.py:107
  6.3 0.6 collective-permute-start
  8.7 0.7 fusion.39
  9.4 0.6 compare_convert_fusion.1
  10.9 0.8 fusion.37
  11.8 0.9 pad_maximum_fusion.2
  12.7 4.7 %all-to-all-start = ((bf16[4,2,64,1,512]{4,2,1,3,0:T(8,128)(2,1)}), bf16[4,2,64,1,512]{4,2,1,3,0:T(8,128)(2,1)S(1)}, u32[]{:S(2)}, u32[]{:S(2)}) async-start(bf16[4,2,64,1,512]{4,2,1,3,0:T(8,128)(2,1)} %pad_maximum_fusion.2), calls=%async_computation | async-start | bytes 1048576 | tf_op jit(solution)/shard_map/all_to_all | solution.py:15
  17.5 1.1 %copy.132 = bf16[2,8,4,8,1024]{4,3,1,0,2:T(8,128)(2,1)} copy(bf16[2,8,4,8,1024]{4,3,2,1,0:T(8,128)(2,1)S(1)} %bitcast.118) | data formatting | bytes 2097152 | tf_op jit(solution)/shard_map/reshape | solution.py:45
  18.6 7.5 %all-to-all-done = bf16[4,2,64,1,512]{4,2,1,3,0:T(8,128)(2,1)S(1)} async-done(((bf16[4,2,64,1,512]{4,2,1,3,0:T(8,128)(2,1)}), bf16[4,2,64,1,512]{4,2,1,3,0:T(8,128)(2,1)S(1)}, u32[]{:S(2)}, u32[]{:S(2)}) %all-to-all-start) | async-done | bytes 524320 | tf_op jit(solution)/shard_map/all_to_all | solution.py:15
  26.1 3.5 %all-to-all-start.1 = ((bf16[2,64,4,1024]{3,1,0,2:T(8,128)(2,1)}), bf16[2,64,4,1024]{3,1,0,2:T(8,128)(2,1)S(1)}, u32[]{:S(2)}, u32[]{:S(2)}) async-start(bf16[2,64,4,1024]{3,1,0,2:T(8,128)(2,1)} %bitcast.116), calls=%async_computation.1 | async-start | bytes 2097152 | tf_op jit(solution)/shard_map/all_to_all | solution.py:55
  29.6 0.7 compare_convert_fusion
  31.0 12.0 %all-to-all-done.1 = bf16[2,64,4,1024]{3,1,0,2:T(8,128)(2,1)S(1)} async-done(((bf16[2,64,4,1024]{3,1,0,2:T(8,128)(2,1)}), bf16[2,64,4,1024]{3,1,0,2:T(8,128)(2,1)S(1)}, u32[]{:S(2)}, u32[]{:S(2)}) %all-to-all-start.1) | async-done | bytes 1048608 | tf_op jit(solution)/shard_map/all_to_all | solution.py:55
  43.1 0.4 reshape_squeeze.20
  43.5 0.5 fusion.26
  43.9 0.9 fusion.41
  45.5 0.4 convert_element_type.63
  45.9 0.4 reshape_squeeze.23
  46.2 0.5 fusion.24
  46.7 0.9 fusion.40
  48.8 16.1 %all_to_all.38 = bf16[2,4,64,1024]{3,2,0,1:T(8,128)(2,1)S(1)} all-to-all(bf16[2,4,64,1024]{3,2,0,1:T(8,128)(2,1)S(1)} %copy.105), channel_id=1, replica_groups=mesh['section'=4,'dp'=2,'seq'=4] {'seq'}, dimensions={1} | all-to-all | bytes 2097152 | tf_op jit(solution)/shard_map/all_to_all | solution.py:114
  65.0 1.6 %collective-permute-start.1 = (bf16[2,1,64,4096]{3,2,0,1:T(8,128)(2,1)S(1)}, bf16[2,1,64,4096]{3,2,0,1:T(8,128)(2,1)S(1)}, u32[]{:S(2)}, u32[]{:S(2)}) collective-permute-start(bf16[2,1,64,4096]{3,2,0,1:T(8,128)(2,1)S(1)} %bitcast.122), channel_id=1, source_target_pairs={{0,8},{8,16},{16,24},{24,0},{1,9},{9,17},{17,25},{25,1},{2,10},{10... | collective-permute-start | bytes 3145736 | tf_op jit(solution)/shard_map/ppermute | solution.py:32
  66.6 22.9 %collective-permute-done.1 = bf16[2,1,64,4096]{3,2,0,1:T(8,128)(2,1)S(1)} collective-permute-done((bf16[2,1,64,4096]{3,2,0,1:T(8,128)(2,1)S(1)}, bf16[2,1,64,4096]{3,2,0,1:T(8,128)(2,1)S(1)}, u32[]{:S(2)}, u32[]{:S(2)}) %collective-permute-start.1) | collective-permute-done | bytes 1048608 | tf_op jit(solution)/shard_map/ppermute | solution.py:32
  89.5 1.0 %copy.135 = bf16[1,2,64,4096]{3,2,1,0:T(8,128)(2,1)} copy(bf16[1,2,64,4096]{3,2,1,0:T(8,128)(2,1)S(1)} %bitcast.123) | data formatting | bytes 2097152
  (37 shorter events, 4.1 us)
Async XLA Ops:
  0.0 7.6 %copy-start = (s32[1,4,8]{2,1,0:T(4,128)S(1)}, s32[1,4,8]{2,1,0:T(4,128)}, u32[]{:S(2)}) copy-start(s32[1,4,8]{2,1,0:T(4,128)} %param.6) | copy-start | bytes 388
  0.0 8.5 %copy-start.1 = (s32[1,4]{1,0:T(1,128)S(1)}, s32[1,4]{1,0:T(1,128)}, u32[]{:S(2)}) copy-start(s32[1,4]{1,0:T(1,128)} %param.5) | copy-start | bytes 52
  6.3 3.9 %collective-permute-start = (bf16[1,64,6144]{2,1,0:T(8,128)(2,1)S(1)}, bf16[1,64,6144]{2,1,0:T(8,128)(2,1)S(1)}, u32[]{:S(2)}, u32[]{:S(2)}) collective-permute-start(bf16[1,64,6144]{2,1,0:T(8,128)(2,1)S(1)} %get-tuple-element.8), channel_id=1, source_target_pairs={{0,4},{4,0},{1,5},{5,1},{2,6},{6,2},{3,7},{7,3},{8,12},{12,8},{9,1... | collective-permute-start | bytes 2359304 | tf_op jit(solution)/shard_map/ppermute | solution.py:26
  12.7 13.4 %all-to-all-start = ((bf16[4,2,64,1,512]{4,2,1,3,0:T(8,128)(2,1)}), bf16[4,2,64,1,512]{4,2,1,3,0:T(8,128)(2,1)S(1)}, u32[]{:S(2)}, u32[]{:S(2)}) async-start(bf16[4,2,64,1,512]{4,2,1,3,0:T(8,128)(2,1)} %pad_maximum_fusion.2), calls=%async_computation | async-start | bytes 1048576 | tf_op jit(solution)/shard_map/all_to_all | solution.py:15
  26.1 16.9 %all-to-all-start.1 = ((bf16[2,64,4,1024]{3,1,0,2:T(8,128)(2,1)}), bf16[2,64,4,1024]{3,1,0,2:T(8,128)(2,1)S(1)}, u32[]{:S(2)}, u32[]{:S(2)}) async-start(bf16[2,64,4,1024]{3,1,0,2:T(8,128)(2,1)} %bitcast.116), calls=%async_computation.1 | async-start | bytes 2097152 | tf_op jit(solution)/shard_map/all_to_all | solution.py:55
  65.0 24.5 %collective-permute-start.1 = (bf16[2,1,64,4096]{3,2,0,1:T(8,128)(2,1)S(1)}, bf16[2,1,64,4096]{3,2,0,1:T(8,128)(2,1)S(1)}, u32[]{:S(2)}, u32[]{:S(2)}) collective-permute-start(bf16[2,1,64,4096]{3,2,0,1:T(8,128)(2,1)S(1)} %bitcast.122), channel_id=1, source_target_pairs={{0,8},{8,16},{16,24},{24,0},{1,9},{9,17},{17,25},{25,1},{2,10},{10... | collective-permute-start | bytes 3145736 | tf_op jit(solution)/shard_map/ppermute | solution.py:32
